TPU v7x, 256 devices: a whole 4x4x8 slice. The times are simulated.
256 devices in a mesh: blk: 128 (over z, x, y_hi, core), pair: 2 (over y_lo).
Axes of the slice: x: 4, y: 4 (y_hi: 2, y_lo: 2; y = y_hi * 2 + y_lo), z: 8, core: 2. Of those that a mesh axis runs over, the one named last changes fastest.
Arguments:
- images: bfloat16 [114688, 768], P(('blk', 'pair')), may hold values from -1 to 1
- texts: bfloat16 [114688, 768], P(('blk', 'pair')), may hold values from -1 to 1
- scale: float32 [], replicated, may hold values from 4 to 16
- bias: float32 [], replicated, may hold values from -6 to -2
Outputs:
- row_loss: float32 [114688], P(('blk', 'pair'))
- grad_images: float32 [114688, 768], P(('blk', 'pair'))
- grad_texts: float32 [114688, 768], P(('blk', 'pair'))
All inputs are finite; a program needn't handle non-finite values.
Results may differ from a plain program's by a relative error of at most 0.0056.
Values may be sent and summed in bfloat16 or wider, within the bound.
No kernel may reach another device: no remote copies, remote signals or barrier semaphores. Data moves between devices by JAX's collectives and lax.ppermute only.
A program may use at most 128 MiB of HBM per device.

v0:
```python
import jax
import jax.numpy as jnp
from jax import lax
from jax.sharding import PartitionSpec as P

STEPS = 6


EPSILON = 1e-06


def passed_along(block, axis, distance):
    devices = range(lax.axis_size(axis))
    route = [((i - distance) % len(devices), i) for i in devices]
    return lax.ppermute(block, axis, route)


def unit_rows(features):
    widened = features.astype(jnp.float32)
    inverse = lax.rsqrt(jnp.sum(widened * widened, axis=1, keepdims=True) + EPSILON)
    return (widened * inverse, inverse)


def tangent(unit, inverse, direction):
    return inverse * (direction - unit * jnp.sum(unit * direction, axis=1, keepdims=True))


def make_labels(logits, offset, row_count):
    if offset == 0:
        column = lax.broadcasted_iota(jnp.int32, logits.shape, 1)
        target = (
            lax.broadcasted_iota(jnp.int32, logits.shape, 0) + lax.axis_index("pair") * row_count
        )
        return jnp.where(column == target, 1.0, -1.0).astype(jnp.float32)
    return -1.0


def move_partials(partial_rows, steps_by):
    return passed_along(partial_rows, "blk", steps_by)


def visit(image_emb, text_now, offset, scale, bias):
    logits = (
        scale
        * lax.dot_general(
            image_emb, text_now, (((1,), (1,)), ((), ())), preferred_element_type=jnp.float32
        )
        + bias
    )
    labels = make_labels(logits, offset, image_emb.shape[0])
    margin = labels * logits
    loss_rows = jnp.sum(jax.nn.softplus(-margin), axis=1)
    weights_bf = (scale * -labels * jax.nn.sigmoid(-margin)).astype(jnp.bfloat16)
    image_grad = jnp.dot(weights_bf, text_now, preferred_element_type=jnp.float32)
    text_grad = None
    text_grad = lax.dot_general(
        weights_bf, image_emb, (((0,), (0,)), ((), ())), preferred_element_type=jnp.float32
    )
    text_grad = lax.psum_scatter(text_grad, "pair", scatter_dimension=0, tiled=True)
    return (loss_rows, image_grad, text_grad)


def body(images, texts, scale, bias):
    image_unit, image_inverse = unit_rows(images)
    text_unit, text_inverse = unit_rows(texts)
    image_emb = image_unit.astype(jnp.bfloat16)
    text_emb = text_unit.astype(jnp.bfloat16)
    text_now = lax.all_gather(text_emb, "pair", axis=0, tiled=True)
    loss_total = jnp.zeros((images.shape[0],), jnp.float32)
    image_dir = jnp.zeros(images.shape, jnp.float32)
    partial_value = None
    for offset in range(STEPS):
        next_text = passed_along(text_now, "blk", 1) if offset + 1 < STEPS else text_now
        loss_rows, image_grad, text_grad = visit(image_emb, text_now, offset, scale, bias)
        loss_total = loss_total + loss_rows
        image_dir = image_dir + image_grad
        partial_value = text_grad if offset == 0 else partial_value + text_grad
        if offset + 1 < STEPS:
            partial_value = move_partials(partial_value, 1)
        text_now = next_text
    partial_value = move_partials(partial_value, 1 - STEPS)
    window = STEPS * lax.axis_size("pair") * images.shape[0]
    row_loss = loss_total / window
    grad_images = tangent(image_unit, image_inverse, image_dir)
    grad_texts = tangent(text_unit, text_inverse, partial_value)
    return (row_loss, grad_images, grad_texts)


def solution(mesh):
    in_specs = (P(("blk", "pair"), None), P(("blk", "pair"), None), P(), P())
    out_specs = (P(("blk", "pair")), P(("blk", "pair"), None), P(("blk", "pair"), None))
    return jax.shard_map(body, mesh=mesh, in_specs=in_specs, out_specs=out_specs, check_vma=False)
```

profile of v0, /device:TPU:103, one launch (start us, length us, event | category | flops | bytes accessed | tf_op | source)
XLA Modules:
  0.0 489.4 jit_solution(828108794083541153)
XLA Ops:
  7.2 1.4 fusion.22
  8.6 2.1 fusion.2
  10.8 0.0 reduce-scatter.7.cloned.1.call-start
  12.1 0.2 fusion.18
  12.3 30.3 %all-gather.2.cloned.1.call-done = bf16[896,768]{1,0:T(8,128)(2,1)} async-done(((bf16[448,768]{1,0:T(8,128)(2,1)}), bf16[896,768]{1,0:T(8,128)(2,1)}) %all-gather.2.cloned.1.call-update) | async-done | bytes 1376272 | tf_op jit(solution)/shard_map/all_gather | solution.py:68
  42.6 3.6 fusion.8
  46.3 0.9 copy-done.2
  47.1 2.5 fusion.33
  49.7 0.0 reduce-scatter.9.cloned.1.call-start
  49.7 1.3 copy-done.4
  51.0 3.2 collective-permute-start
  54.2 29.3 %collective-permute-done = bf16[896,768]{1,0:T(8,128)(2,1)S(1)} collective-permute-done((bf16[896,768]{1,0:T(8,128)(2,1)S(1)}, bf16[896,768]{1,0:T(8,128)(2,1)S(1)}, u32[]{:S(2)}, u32[]{:S(2)}) %collective-permute-start) | collective-permute-done | bytes 1376288 | tf_op jit(solution)/shard_map/ppermute | solution.py:15
  83.4 2.6 fusion.10
  86.1 4.0 fusion.23
  90.2 4.1 collective-permute-start.1
  94.3 19.4 %collective-permute-done.1 = bf16[896,768]{1,0:T(8,128)(2,1)S(1)} collective-permute-done((bf16[896,768]{1,0:T(8,128)(2,1)S(1)}, bf16[896,768]{1,0:T(8,128)(2,1)S(1)}, u32[]{:S(2)}, u32[]{:S(2)}) %collective-permute-start.1) | collective-permute-done | bytes 1376288 | tf_op jit(solution)/shard_map/ppermute | solution.py:15
  113.7 1.7 fusion.11
  115.3 1.2 copy-done.16
  116.5 2.6 fusion.24
  119.1 0.0 reduce-scatter.13.cloned.1.call-start
  119.2 4.2 collective-permute-start.2
  123.4 15.3 %collective-permute-done.2 = bf16[896,768]{1,0:T(8,128)(2,1)S(1)} collective-permute-done((bf16[896,768]{1,0:T(8,128)(2,1)S(1)}, bf16[896,768]{1,0:T(8,128)(2,1)S(1)}, u32[]{:S(2)}, u32[]{:S(2)}) %collective-permute-start.2) | collective-permute-done | bytes 1376288 | tf_op jit(solution)/shard_map/ppermute | solution.py:15
  138.7 1.7 fusion.12
  140.4 1.2 copy-done.18
  141.5 2.6 fusion.25
  144.3 4.1 collective-permute-start.3
  148.3 41.2 %collective-permute-done.3 = bf16[896,768]{1,0:T(8,128)(2,1)S(1)} collective-permute-done((bf16[896,768]{1,0:T(8,128)(2,1)S(1)}, bf16[896,768]{1,0:T(8,128)(2,1)S(1)}, u32[]{:S(2)}, u32[]{:S(2)}) %collective-permute-start.3) | collective-permute-done | bytes 1376288 | tf_op jit(solution)/shard_map/ppermute | solution.py:15
  189.5 1.7 fusion.13
  191.2 1.2 copy-done.20
  192.4 2.7 fusion.26
  195.1 0.0 reduce-scatter.17.cloned.1.call-start
  195.2 1.3 copy-done.13
  196.4 4.0 collective-permute-start.4
  200.4 15.2 %collective-permute-done.4 = bf16[896,768]{1,0:T(8,128)(2,1)} collective-permute-done((bf16[896,768]{1,0:T(8,128)(2,1)S(1)}, bf16[896,768]{1,0:T(8,128)(2,1)}, u32[]{:S(2)}, u32[]{:S(2)}) %collective-permute-start.4) | collective-permute-done | bytes 1376288 | tf_op jit(solution)/shard_map/ppermute | solution.py:15
  215.7 4.0 fusion.14
  219.7 10.8 %collective-permute-done.5 = f32[448,768]{1,0:T(8,128)S(1)} collective-permute-done((f32[448,768]{1,0:T(8,128)}, f32[448,768]{1,0:T(8,128)S(1)}, u32[]{:S(2)}, u32[]{:S(2)}) %collective-permute-start.5) | collective-permute-done | bytes 1376288 | tf_op jit(solution)/shard_map/ppermute | solution.py:15
  230.5 1.6 add.176
  232.1 4.0 collective-permute-start.6
  236.1 2.6 fusion.27
  238.7 42.2 %reduce-scatter.11.cloned.1.call-done = f32[448,768]{1,0:T(8,128)} async-done(((f32[896,768]{1,0:T(8,128)}), f32[448,768]{1,0:T(8,128)}) %reduce-scatter.11.cloned.1.call-update) | async-done | bytes 1376272 | tf_op jit(solution)/shard_map/reduce_scatter | solution.py:59
  280.9 1.5 add.177
  282.4 2.1 collective-permute-start.7
  284.5 48.1 %reduce-scatter.13.cloned.1.call-done = f32[448,768]{1,0:T(8,128)} async-done(((f32[896,768]{1,0:T(8,128)}), f32[448,768]{1,0:T(8,128)}) %reduce-scatter.13.cloned.1.call-update) | async-done | bytes 1376272 | tf_op jit(solution)/shard_map/reduce_scatter | solution.py:59
  332.6 1.6 add.178
  334.2 3.4 collective-permute-start.8
  337.6 2.0 fusion.41
  339.6 45.0 %reduce-scatter.15.cloned.1.call-done = f32[448,768]{1,0:T(8,128)} async-done(((f32[896,768]{1,0:T(8,128)}), f32[448,768]{1,0:T(8,128)}) %reduce-scatter.15.cloned.1.call-update) | async-done | bytes 1376272 | tf_op jit(solution)/shard_map/reduce_scatter | solution.py:59
  384.6 1.6 add.179
  386.2 2.7 collective-permute-start.9
  389.0 2.5 convolution_add_fusion.4
  391.5 1.0 convolution_add_fusion.3
  392.5 0.3 copy-done.11
  392.8 0.5 copy-done.19
  393.3 2.1 convolution_add_fusion.2
  395.4 40.4 %reduce-scatter.17.cloned.1.call-done = f32[448,768]{1,0:T(8,128)} async-done(((f32[896,768]{1,0:T(8,128)}), f32[448,768]{1,0:T(8,128)}) %reduce-scatter.17.cloned.1.call-update) | async-done | bytes 1376272 | tf_op jit(solution)/shard_map/reduce_scatter | solution.py:59
  435.9 1.6 add.180
  437.5 1.2 collective-permute-start.10
  438.7 2.4 convolution_add_fusion.1
  441.1 0.6 add_multiply_fusion.5
  441.7 2.5 fusion.15
  444.2 1.4 fusion.17
  445.6 35.2 %collective-permute-done.10 = f32[448,768]{1,0:T(8,128)S(1)} collective-permute-done((f32[448,768]{1,0:T(8,128)S(1)}, f32[448,768]{1,0:T(8,128)S(1)}, u32[]{:S(2)}, u32[]{:S(2)}) %collective-permute-start.10) | collective-permute-done | bytes 1376288 | tf_op jit(solution)/shard_map/ppermute | solution.py:15
  480.8 0.3 fusion.19
  481.2 1.4 fusion.21
  (60 shorter events, 0.4 us)
Async XLA Ops:
  7.2 5.0 %copy-start.1 = (bf16[448,768]{1,0:T(8,128)(2,1)S(1)}, bf16[448,768]{1,0:T(8,128)(2,1)}, u32[]{:S(2)}) copy-start(bf16[448,768]{1,0:T(8,128)(2,1)} %param.4) | copy-start | bytes 2064388
  7.2 35.4 %all-gather.2.cloned.1.call-start = ((), (), s32[]{:S(2)}) async-start(), calls=%async_computation.6 | async-start | bytes 2064384 | tf_op jit(solution)/shard_map/all_gather | solution.py:68
  10.8 189.7 %reduce-scatter.7.cloned.1.call-start = ((), (), s32[]{:S(2)}) async-start(), calls=%async_computation.7 | async-start | bytes 4128768 | tf_op jit(solution)/shard_map/reduce_scatter | solution.py:59
  46.2 0.9 copy-start.2
  49.7 1.3 copy-start.4
  49.7 180.8 %reduce-scatter.9.cloned.1.call-start = ((), (), s32[]{:S(2)}) async-start(), calls=%async_computation.8 | async-start | bytes 4128768 | tf_op jit(solution)/shard_map/reduce_scatter | solution.py:59
  51.0 32.4 %collective-permute-start = (bf16[896,768]{1,0:T(8,128)(2,1)S(1)}, bf16[896,768]{1,0:T(8,128)(2,1)S(1)}, u32[]{:S(2)}, u32[]{:S(2)}) collective-permute-start(bf16[896,768]{1,0:T(8,128)(2,1)S(1)} %copy-done.4), channel_id=1, source_target_pairs={{254,0},{0,2},{2,4},{4,6},{6,8},{8,10},{10,12},{12,14},{14,16},{16... | collective-permute-start | bytes 4128776 | tf_op jit(solution)/shard_map/ppermute | solution.py:15
  83.4 6.8 %copy-start.6 = (bf16[896,768]{1,0:T(8,128)(2,1)}, bf16[896,768]{1,0:T(8,128)(2,1)S(1)}, u32[]{:S(2)}) copy-start(bf16[896,768]{1,0:T(8,128)(2,1)S(1)} %collective-permute-done) | copy-start | bytes 4128772
  90.1 190.8 %reduce-scatter.11.cloned.1.call-start = ((), (), s32[]{:S(2)}) async-start(), calls=%async_computation.9 | async-start | bytes 4128768 | tf_op jit(solution)/shard_map/reduce_scatter | solution.py:59
  90.2 23.5 %collective-permute-start.1 = (bf16[896,768]{1,0:T(8,128)(2,1)S(1)}, bf16[896,768]{1,0:T(8,128)(2,1)S(1)}, u32[]{:S(2)}, u32[]{:S(2)}) collective-permute-start(bf16[896,768]{1,0:T(8,128)(2,1)S(1)} %collective-permute-done), channel_id=1, source_target_pairs={{254,0},{0,2},{2,4},{4,6},{6,8},{8,10},{10,12},{12,14},{14,16},{16... | collective-permute-start | bytes 4128776 | tf_op jit(solution)/shard_map/ppermute | solution.py:15
  113.7 5.5 %copy-start.8 = (bf16[896,768]{1,0:T(8,128)(2,1)}, bf16[896,768]{1,0:T(8,128)(2,1)S(1)}, u32[]{:S(2)}) copy-start(bf16[896,768]{1,0:T(8,128)(2,1)S(1)} %collective-permute-done.1) | copy-start | bytes 4128772
  115.3 1.2 copy-start.16
  119.1 213.5 %reduce-scatter.13.cloned.1.call-start = ((), (), s32[]{:S(2)}) async-start(), calls=%async_computation.10 | async-start | bytes 4128768 | tf_op jit(solution)/shard_map/reduce_scatter | solution.py:59
  119.2 19.5 %collective-permute-start.2 = (bf16[896,768]{1,0:T(8,128)(2,1)S(1)}, bf16[896,768]{1,0:T(8,128)(2,1)S(1)}, u32[]{:S(2)}, u32[]{:S(2)}) collective-permute-start(bf16[896,768]{1,0:T(8,128)(2,1)S(1)} %collective-permute-done.1), channel_id=1, source_target_pairs={{254,0},{0,2},{2,4},{4,6},{6,8},{8,10},{10,12},{12,14},{14,16},{16... | collective-permute-start | bytes 4128776 | tf_op jit(solution)/shard_map/ppermute | solution.py:15
  138.7 5.6 %copy-start.10 = (bf16[896,768]{1,0:T(8,128)(2,1)}, bf16[896,768]{1,0:T(8,128)(2,1)S(1)}, u32[]{:S(2)}) copy-start(bf16[896,768]{1,0:T(8,128)(2,1)S(1)} %collective-permute-done.2) | copy-start | bytes 4128772
  140.3 1.2 copy-start.18
  144.2 240.4 %reduce-scatter.15.cloned.1.call-start = ((), (), s32[]{:S(2)}) async-start(), calls=%async_computation.11 | async-start | bytes 4128768 | tf_op jit(solution)/shard_map/reduce_scatter | solution.py:59
  144.3 45.3 %collective-permute-start.3 = (bf16[896,768]{1,0:T(8,128)(2,1)S(1)}, bf16[896,768]{1,0:T(8,128)(2,1)S(1)}, u32[]{:S(2)}, u32[]{:S(2)}) collective-permute-start(bf16[896,768]{1,0:T(8,128)(2,1)S(1)} %collective-permute-done.2), channel_id=1, source_target_pairs={{254,0},{0,2},{2,4},{4,6},{6,8},{8,10},{10,12},{12,14},{14,16},{16... | collective-permute-start | bytes 4128776 | tf_op jit(solution)/shard_map/ppermute | solution.py:15
  189.5 1.7 copy-start.12
  191.2 1.2 copy-start.20
  195.1 1.3 copy-start.13
  195.1 240.8 %reduce-scatter.17.cloned.1.call-start = ((), (), s32[]{:S(2)}) async-start(), calls=%async_computation.12 | async-start | bytes 4128768 | tf_op jit(solution)/shard_map/reduce_scatter | solution.py:59
  196.4 19.2 %collective-permute-start.4 = (bf16[896,768]{1,0:T(8,128)(2,1)S(1)}, bf16[896,768]{1,0:T(8,128)(2,1)}, u32[]{:S(2)}, u32[]{:S(2)}) collective-permute-start(bf16[896,768]{1,0:T(8,128)(2,1)S(1)} %copy-done.13), channel_id=1, source_target_pairs={{254,0},{0,2},{2,4},{4,6},{6,8},{8,10},{10,12},{12,14},{14,16},{16... | collective-permute-start | bytes 4128776 | tf_op jit(solution)/shard_map/ppermute | solution.py:15
  200.4 30.1 %collective-permute-start.5 = (f32[448,768]{1,0:T(8,128)}, f32[448,768]{1,0:T(8,128)S(1)}, u32[]{:S(2)}, u32[]{:S(2)}) collective-permute-start(f32[448,768]{1,0:T(8,128)} %reduce-scatter.7.cloned.1.call-done), channel_id=1, source_target_pairs={{254,0},{0,2},{2,4},{4,6},{6,8},{8,10},{10,12},{12,14},{14,16},{16... | collective-permute-start | bytes 4128776 | tf_op jit(solution)/shard_map/ppermute | solution.py:15
  230.5 5.6 %copy-start.22 = (f32[448,896]{1,0:T(8,128)S(1)}, f32[448,896]{1,0:T(8,128)}, u32[]{:S(2)}) copy-start(f32[448,896]{1,0:T(8,128)} %get-tuple-element.6) | copy-start | bytes 4816900
  232.1 48.8 %collective-permute-start.6 = (f32[448,768]{1,0:T(8,128)S(1)}, f32[448,768]{1,0:T(8,128)S(1)}, u32[]{:S(2)}, u32[]{:S(2)}) collective-permute-start(f32[448,768]{1,0:T(8,128)S(1)} %add.176), channel_id=1, source_target_pairs={{254,0},{0,2},{2,4},{4,6},{6,8},{8,10},{10,12},{12,14},{14,16},{16... | collective-permute-start | bytes 4128776 | tf_op jit(solution)/shard_map/ppermute | solution.py:15
  282.4 50.2 %collective-permute-start.7 = (f32[448,768]{1,0:T(8,128)S(1)}, f32[448,768]{1,0:T(8,128)S(1)}, u32[]{:S(2)}, u32[]{:S(2)}) collective-permute-start(f32[448,768]{1,0:T(8,128)S(1)} %add.177), channel_id=1, source_target_pairs={{254,0},{0,2},{2,4},{4,6},{6,8},{8,10},{10,12},{12,14},{14,16},{16... | collective-permute-start | bytes 4128776 | tf_op jit(solution)/shard_map/ppermute | solution.py:15
  332.6 5.0 %copy-start.3 = (bf16[448,896]{1,0:T(8,128)(2,1)S(1)}, bf16[448,896]{1,0:T(8,128)(2,1)}, u32[]{:S(2)}) copy-start(bf16[448,896]{1,0:T(8,128)(2,1)} %copy-done.2) | copy-start | bytes 2408452
  332.6 5.0 %copy-start.5 = (bf16[896,768]{1,0:T(8,128)(2,1)S(1)}, bf16[896,768]{1,0:T(8,128)(2,1)}, u32[]{:S(2)}) copy-start(bf16[896,768]{1,0:T(8,128)(2,1)} %all-gather.2.cloned.1.call-done) | copy-start | bytes 4128772
  334.2 50.4 %collective-permute-start.8 = (f32[448,768]{1,0:T(8,128)S(1)}, f32[448,768]{1,0:T(8,128)S(1)}, u32[]{:S(2)}, u32[]{:S(2)}) collective-permute-start(f32[448,768]{1,0:T(8,128)S(1)} %add.178), channel_id=1, source_target_pairs={{254,0},{0,2},{2,4},{4,6},{6,8},{8,10},{10,12},{12,14},{14,16},{16... | collective-permute-start | bytes 4128776 | tf_op jit(solution)/shard_map/ppermute | solution.py:15
  384.6 4.4 copy-start.7
  384.6 4.4 copy-start.15
  386.2 5.2 %copy-start.9 = (bf16[896,768]{1,0:T(8,128)(2,1)S(1)}, bf16[896,768]{1,0:T(8,128)(2,1)}, u32[]{:S(2)}) copy-start(bf16[896,768]{1,0:T(8,128)(2,1)} %copy-done.8) | copy-start | bytes 4128772
  386.2 5.2 %copy-start.17 = (f32[448,896]{1,0:T(8,128)S(1)}, f32[448,896]{1,0:T(8,128)}, u32[]{:S(2)}) copy-start(f32[448,896]{1,0:T(8,128)} %copy-done.16) | copy-start | bytes 4816900
  386.2 49.6 %collective-permute-start.9 = (f32[448,768]{1,0:T(8,128)S(1)}, f32[448,768]{1,0:T(8,128)S(1)}, u32[]{:S(2)}, u32[]{:S(2)}) collective-permute-start(f32[448,768]{1,0:T(8,128)S(1)} %add.179), channel_id=1, source_target_pairs={{254,0},{0,2},{2,4},{4,6},{6,8},{8,10},{10,12},{12,14},{14,16},{16... | collective-permute-start | bytes 4128776 | tf_op jit(solution)/shard_map/ppermute | solution.py:15
  391.5 1.3 copy-start.11
  391.5 1.8 copy-start.19
  435.9 2.9 copy-start.14
  435.9 2.9 copy-start.21
  437.5 4.2 copy-start.23
  437.5 43.3 %collective-permute-start.10 = (f32[448,768]{1,0:T(8,128)S(1)}, f32[448,768]{1,0:T(8,128)S(1)}, u32[]{:S(2)}, u32[]{:S(2)}) collective-permute-start(f32[448,768]{1,0:T(8,128)S(1)} %add.180), channel_id=1, source_target_pairs={{10,0},{12,2},{14,4},{16,6},{18,8},{20,10},{22,12},{24,14},{26,16}... | collective-permute-start | bytes 4128776 | tf_op jit(solution)/shard_map/ppermute | solution.py:15
  444.2 36.6 %copy-start = (bf16[448,768]{1,0:T(8,128)(2,1)S(1)}, bf16[448,768]{1,0:T(8,128)(2,1)}, u32[]{:S(2)}) copy-start(bf16[448,768]{1,0:T(8,128)(2,1)} %param.5) | copy-start | bytes 2064388
Sparse Core Ops, SparseCore 0:
  10.9 31.6 all-gather.1
  49.8 54.4 reduce-scatter.6
  106.8 84.5 reduce-scatter.8
  193.7 87.1 reduce-scatter.10
  283.3 49.2 reduce-scatter.12
  334.9 49.5 reduce-scatter.14
  387.1 48.7 reduce-scatter.16
where the time goes:
time: 490 us; the launch traced here: 489 us
  waiting for transfers between devices  373 us (76%)
  matrix products  44.9 us (9%)
  starting transfers between devices  33.2 us (7%)
  between operations  15.6 us (3%)
  other arithmetic  15.4 us (3%)
  local copies, waits for them, and re-layouts  7.78 us (2%)
    reduce_scatter x6, waiting for transfers between devices, visit(): lax.psum_scatter(text_grad, 'pair', scatter_dimension=0, tiled=True)  176 us
    ppermute x11, waiting for transfers between devices, passed_along(): return lax.ppermute(block, axis, route)  166 us
    ppermute x11, starting transfers between devices, passed_along(): return lax.ppermute(block, axis, route)  32.9 us
    all_gather x1, waiting for transfers between devices, body(): text_now = lax.all_gather(text_emb, 'pair', axis=0, tiled=True)  30.3 us
    dot_general x6, matrix products, visit(): lax.dot_general(weights_bf, image_emb, (((0,), (0,)), ((), ())), preferre...  17.1 us
    dot_general x6, matrix products, visit(): lax.dot_general(image_emb, text_now, (((1,), (1,)), ((), ())), preferred_...  15.3 us
    dot_general x6, matrix products, visit(): jnp.dot(weights_bf, text_now, preferred_element_type=jnp.float32)  12.5 us
  transfers between devices with their start and end apart: 18, of which 12 were waited for; matrix products, arithmetic and copies ran while one was open for 10% of the time, Pallas kernels for 0%

commit v1 on v0

v1 whole, which is shorter than its diff:
```python
import jax
import jax.numpy as jnp
import numpy as np
from jax import lax
from jax.sharding import PartitionSpec as P

STEPS = 6


EPSILON = 1e-06


def unit_rows(features):
    widened = features.astype(jnp.float32)
    inverse = lax.rsqrt(jnp.sum(widened * widened, axis=1, keepdims=True) + EPSILON)
    return (widened * inverse, inverse)


def tangent(unit, inverse, direction):
    return inverse * (direction - unit * jnp.sum(unit * direction, axis=1, keepdims=True))


def device_coords(mesh):
    try:
        devices = mesh.devices
        return np.array([[d.coords for d in row] for row in devices])
    except Exception:
        return None


def hops(coords, shape, a, b):
    if coords is None:
        return 0
    delta = np.abs(coords[a] - coords[b])
    return int(np.sum(np.minimum(delta, np.array(shape) - delta)))


def group_routes(mesh, shift):
    n_blk, n_pair = mesh.shape["blk"], mesh.shape["pair"]
    coords = device_coords(mesh)
    shape = None
    if coords is not None:
        shape = tuple(int(v) + 1 for v in coords.reshape(-1, 3).max(axis=0))
    route = []
    for g in range(n_blk):
        h = (g + shift) % n_blk
        same = sum(hops(coords, shape, (g, p), (h, p)) for p in range(n_pair))
        cross = sum(hops(coords, shape, (g, p), (h, n_pair - 1 - p)) for p in range(n_pair))
        for p in range(n_pair):
            q = p if same <= cross else n_pair - 1 - p
            route.append((g * n_pair + p, h * n_pair + q))
    return route


def score(mine, block, diagonal, scale, bias):
    logits = (
        scale
        * lax.dot_general(
            mine, block, (((1,), (1,)), ((), ())), preferred_element_type=jnp.float32
        )
        + bias
    )
    if diagonal:
        column = lax.broadcasted_iota(jnp.int32, logits.shape, 1)
        target = lax.broadcasted_iota(jnp.int32, logits.shape, 0) + lax.axis_index("pair") * mine.shape[0]
        labels = jnp.where(column == target, 1.0, -1.0).astype(jnp.float32)
    else:
        labels = -1.0
    margin = labels * logits
    weights_bf = (scale * -labels * jax.nn.sigmoid(-margin)).astype(jnp.bfloat16)
    return margin, weights_bf


def make_body(mesh):
    pair_route = [(i, i ^ 1) for i in range(mesh.shape["blk"] * mesh.shape["pair"])]
    text_routes = [group_routes(mesh, k) for k in range(1, STEPS)]
    image_routes = [group_routes(mesh, -k) for k in range(1, STEPS)]
    axes = ("blk", "pair")

    def body(images, texts, scale, bias):
        rows = images.shape[0]
        image_unit, image_inverse = unit_rows(images)
        text_unit, text_inverse = unit_rows(texts)
        image_emb = image_unit.astype(jnp.bfloat16)
        text_emb = text_unit.astype(jnp.bfloat16)
        mine = jnp.concatenate([text_emb, image_emb], axis=0)
        other = lax.ppermute(mine, axes, pair_route)
        first = lax.axis_index("pair") == 0
        text_group = jnp.where(first, jnp.concatenate([text_emb, other[:rows]], 0),
                               jnp.concatenate([other[:rows], text_emb], 0))
        image_group = jnp.where(first, jnp.concatenate([image_emb, other[rows:]], 0),
                                jnp.concatenate([other[rows:], image_emb], 0))
        text_blocks = [text_group] + [lax.ppermute(text_group, axes, r) for r in text_routes]
        image_blocks = [image_group] + [lax.ppermute(image_group, axes, r) for r in image_routes]
        loss_total = jnp.zeros((rows,), jnp.float32)
        image_dir = jnp.zeros(images.shape, jnp.float32)
        text_dir = jnp.zeros(texts.shape, jnp.float32)
        for offset in range(STEPS):
            margin, weights = score(image_emb, text_blocks[offset], offset == 0, scale, bias)
            loss_total = loss_total + jnp.sum(jax.nn.softplus(-margin), axis=1)
            image_dir = image_dir + jnp.dot(weights, text_blocks[offset], preferred_element_type=jnp.float32)
            _, weights_t = score(text_emb, image_blocks[offset], offset == 0, scale, bias)
            text_dir = text_dir + jnp.dot(weights_t, image_blocks[offset], preferred_element_type=jnp.float32)
        window = STEPS * lax.axis_size("pair") * rows
        row_loss = loss_total / window
        grad_images = tangent(image_unit, image_inverse, image_dir)
        grad_texts = tangent(text_unit, text_inverse, text_dir)
        return (row_loss, grad_images, grad_texts)

    return body


def solution(mesh):
    in_specs = (P(("blk", "pair"), None), P(("blk", "pair"), None), P(), P())
    out_specs = (P(("blk", "pair")), P(("blk", "pair"), None), P(("blk", "pair"), None))
    return jax.shard_map(make_body(mesh), mesh=mesh, in_specs=in_specs, out_specs=out_specs, check_vma=False)
```

time: 490 us -> 234 us (0.48)
  waiting for transfers between devices: 373 us -> 113 us
  matrix products: 44.9 us -> 70.2 us
  between operations: 15.6 us -> 2.09 us
  local copies, waits for them, and re-layouts: 7.78 us -> 1.43 us
    reduce_scatter x6 -> x0, waiting for transfers between devices: 176 us -> none  [visit(): lax.psum_scatter(text_grad, 'pair', scatter_dimension=0, tiled=True)]
    ppermute x11, waiting for transfers between devices: 166 us -> 113 us  [the longest x5 59.3 us: body(): lax.ppermute(image_group, axes, r)]
    all_gather x1 -> x0, waiting for transfers between devices: 30.3 us -> none  [body(): text_now = lax.all_gather(text_emb, 'pair', axis=0, tiled=True)]
    dot_general x18, matrix products: 44.9 us -> 70.2 us  [the longest x6 30.1 us: body(): jnp.dot(weights_t, image_blocks[offset], preferred_element_type=jnp.float32)]
    add x6 -> x1, other arithmetic: 7.94 us -> 0.01 us  [score(): lax.broadcasted_iota(jnp.int32, logits.shape, 0)]
    unnamed x48 -> x14, local copies, waits for them, and re-layouts: 7.78 us -> 0.03 us
  transfers between devices with their start and end apart: 18 -> 11, of which waited for: 12 -> 4; matrix products, arithmetic and copies ran while one was open for 10% -> 30% of each run, Pallas kernels for 0% -> 0%
where the time goes in v1:
time: 234 us; the launch traced here: 231 us
  waiting for transfers between devices  113 us (48%)
  matrix products  70.2 us (30%)
  starting transfers between devices  32.9 us (14%)
  other arithmetic  12.3 us (5%)
    ppermute x5, waiting for transfers between devices, body(): lax.ppermute(image_group, axes, r)  59.3 us
    dot_general x6, matrix products, body(): jnp.dot(weights_t, image_blocks[offset], preferred_element_type=jnp.float32)  30.1 us
    ppermute x1, waiting for transfers between devices, body(): other = lax.ppermute(mine, axes, pair_route)  30.1 us
    ppermute x5, starting transfers between devices, body(): lax.ppermute(text_group, axes, r)  28.4 us
    ppermute x5, waiting for transfers between devices, body(): lax.ppermute(text_group, axes, r)  23.2 us
    dot_general x6, matrix products, score(): lax.dot_general(mine, block, (((1,), (1,)), ((), ())), preferred_element_...  22 us
    dot_general x6, matrix products, body(): jnp.dot(weights, text_blocks[offset], preferred_element_type=jnp.float32)  18.1 us
  transfers between devices with their start and end apart: 11, of which 4 were waited for; matrix products, arithmetic and copies ran while one was open for 30% of the time, Pallas kernels for 0%

profile of v1, /device:TPU:103, one launch (start us, length us, event | category | flops | bytes accessed | tf_op | source)
XLA Modules:
  0.0 231.5 jit_solution(13994138814610504787)
XLA Ops:
  0.6 0.0 copy-start
  0.6 0.0 copy-start.1
  0.7 1.4 fusion.33
  2.1 1.3 fusion.29
  3.4 0.0 copy-done
  3.4 0.0 copy-done.1
  3.4 0.3 fusion.2
  3.7 1.2 pad_maximum_fusion.1
  4.9 1.3 collective-permute-start
  6.2 30.1 %collective-permute-done = bf16[896,768]{1,0:T(8,128)(2,1)} collective-permute-done((bf16[896,768]{1,0:T(8,128)(2,1)}, bf16[896,768]{1,0:T(8,128)(2,1)}, u32[]{:S(2)}, u32[]{:S(2)}) %collective-permute-start) | collective-permute-done | bytes 1376288 | tf_op jit(solution)/shard_map/ppermute | solution.py:87
  36.3 1.4 fusion.93
  37.7 1.7 fusion.25
  39.3 1.5 collective-permute-start.6
  40.9 1.7 fusion.24
  42.5 2.6 %collective-permute-start.1 = (bf16[896,768]{1,0:T(8,128)(2,1)}, bf16[896,768]{1,0:T(8,128)(2,1)}, u32[]{:S(2)}, u32[]{:S(2)}) collective-permute-start(bf16[896,768]{1,0:T(8,128)(2,1)} %fusion.24), channel_id=1, source_target_pairs={{0,2},{1,3},{2,5},{3,4},{4,6},{5,7},{6,9},{7,8},{8,10},{9,11},{10,... | collective-permute-start | bytes 4128776 | tf_op jit(solution)/shard_map/ppermute | solution.py:93
  45.2 0.8 collective-permute-start.8
  47.2 0.3 collective-permute-start.9
  47.6 0.6 collective-permute-start.10
  48.2 4.2 %fusion.14 = (f32[448]{0:T(512)S(1)}, f32[448,896]{1,0:T(8,128)}) fusion(f32[]{:T(128)S(6)} %copy.8, bf16[448,768]{1,0:T(8,128)(2,1)S(1)} %get-tuple-element.22, bf16[896,768]{1,0:T(8,128)(2,1)} %fusion.24, f32[]{:T(128)S(6)} %copy.7, s32[448]{0:T(512)S(1)} %iota_add_fusion), kind=kOutput, calls=%fused_computation.27 | convolution fusion | flops 621780544 | bytes 3673608 | tf_op jit(solution)/shard_map/dot_general | solution.py:58
  52.3 33.1 %collective-permute-done.6 = bf16[896,768]{1,0:T(8,128)(2,1)} collective-permute-done((bf16[896,768]{1,0:T(8,128)(2,1)}, bf16[896,768]{1,0:T(8,128)(2,1)}, u32[]{:S(2)}, u32[]{:S(2)}) %collective-permute-start.6) | collective-permute-done | bytes 1376288 | tf_op jit(solution)/shard_map/ppermute | solution.py:94
  85.4 2.5 %collective-permute-start.3 = (bf16[896,768]{1,0:T(8,128)(2,1)}, bf16[896,768]{1,0:T(8,128)(2,1)}, u32[]{:S(2)}, u32[]{:S(2)}) collective-permute-start(bf16[896,768]{1,0:T(8,128)(2,1)} %fusion.24), channel_id=1, source_target_pairs={{0,7},{1,6},{2,8},{3,9},{4,11},{5,10},{6,12},{7,13},{8,15},{9,14},... | collective-permute-start | bytes 4128776 | tf_op jit(solution)/shard_map/ppermute | solution.py:93
  87.9 4.6 %fusion.36 = f32[448,768]{1,0:T(8,128)} fusion(bf16[896,768]{1,0:T(8,128)(2,1)} %collective-permute-done.6, bf16[448,768]{1,0:T(8,128)(2,1)S(1)} %get-tuple-element.21, f32[]{:T(128)S(6)} %copy.8, f32[]{:T(128)S(6)} %copy.7), kind=kOutput, calls=%fused_computation.72 | convolution fusion | flops 1235935232 | bytes 3440648 | tf_op jit(solution)/shard_map/dot_general | solution.py:103
  92.5 23.1 %collective-permute-done.1 = bf16[896,768]{1,0:T(8,128)(2,1)} collective-permute-done((bf16[896,768]{1,0:T(8,128)(2,1)}, bf16[896,768]{1,0:T(8,128)(2,1)}, u32[]{:S(2)}, u32[]{:S(2)}) %collective-permute-start.1) | collective-permute-done | bytes 1376288 | tf_op jit(solution)/shard_map/ppermute | solution.py:93
  115.7 1.3 collective-permute-start.4
  116.9 3.9 %fusion.15 = (f32[448]{0:T(512)S(1)}, f32[448,896]{1,0:T(8,128)}) fusion(f32[]{:T(128)S(6)} %copy.8, bf16[448,768]{1,0:T(8,128)(2,1)S(1)} %get-tuple-element.22, bf16[896,768]{1,0:T(8,128)(2,1)} %collective-permute-done.1, f32[]{:T(128)S(6)} %copy.7), kind=kOutput, calls=%fused_computation.28 | convolution fusion | flops 620977728 | bytes 3671816 | tf_op jit(solution)/shard_map/dot_general | solution.py:58
  120.9 0.0 collective-permute-done.8
  120.9 0.0 collective-permute-start.7
  120.9 4.7 %fusion.37 = f32[448,768]{1,0:T(8,128)} fusion(bf16[896,768]{1,0:T(8,128)(2,1)} %collective-permute-done.8, bf16[448,768]{1,0:T(8,128)(2,1)S(1)} %get-tuple-element.21, f32[]{:T(128)S(6)} %copy.8, f32[]{:T(128)S(6)} %copy.7), kind=kOutput, calls=%fused_computation.73 | convolution fusion | flops 1235935232 | bytes 3440648 | tf_op jit(solution)/shard_map/dot_general | solution.py:103
  125.6 4.0 %fusion.70 = f32[448,768]{1,0:T(8,128)} fusion(bf16[896,768]{1,0:T(8,128)(2,1)} %collective-permute-done.1, f32[448,896]{1,0:T(8,128)} %get-tuple-element.16, f32[]{:T(128)S(6)} %copy.7), kind=kOutput, calls=%fused_computation.105 | convolution fusion | flops 618168320 | bytes 4358148 | tf_op jit(solution)/shard_map/dot_general | solution.py:101
  129.5 0.0 collective-permute-done.3
  129.5 3.4 %collective-permute-start.5 = (bf16[896,768]{1,0:T(8,128)(2,1)}, bf16[896,768]{1,0:T(8,128)(2,1)}, u32[]{:S(2)}, u32[]{:S(2)}) collective-permute-start(bf16[896,768]{1,0:T(8,128)(2,1)} %fusion.24), channel_id=1, source_target_pairs={{0,10},{1,11},{2,13},{3,12},{4,14},{5,15},{6,17},{7,16},{8,18},{9,... | collective-permute-start | bytes 4128776 | tf_op jit(solution)/shard_map/ppermute | solution.py:93
  132.9 3.0 %fusion.17 = (f32[448]{0:T(512)S(1)}, f32[448,896]{1,0:T(8,128)S(1)}) fusion(f32[]{:T(128)S(6)} %copy.8, bf16[448,768]{1,0:T(8,128)(2,1)S(1)} %get-tuple-element.22, bf16[896,768]{1,0:T(8,128)(2,1)} %collective-permute-done.3, f32[]{:T(128)S(6)} %copy.7), kind=kOutput, calls=%fused_computation.30 | convolution fusion | flops 620977728 | bytes 3671816 | tf_op jit(solution)/shard_map/dot_general | solution.py:58
  135.9 0.0 collective-permute-done.4
  135.9 18.6 %collective-permute-start.2 = (bf16[896,768]{1,0:T(8,128)(2,1)}, bf16[896,768]{1,0:T(8,128)(2,1)}, u32[]{:S(2)}, u32[]{:S(2)}) collective-permute-start(bf16[896,768]{1,0:T(8,128)(2,1)} %fusion.24), channel_id=1, source_target_pairs={{0,5},{1,4},{2,7},{3,6},{4,9},{5,8},{6,11},{7,10},{8,13},{9,12},{1... | collective-permute-start | bytes 4128776 | tf_op jit(solution)/shard_map/ppermute | solution.py:93
  154.5 3.9 %fusion.18 = (f32[448]{0:T(512)S(1)}, f32[448,896]{1,0:T(8,128)}) fusion(f32[]{:T(128)S(6)} %copy.8, bf16[448,768]{1,0:T(8,128)(2,1)S(1)} %get-tuple-element.22, bf16[896,768]{1,0:T(8,128)(2,1)} %collective-permute-done.4, f32[]{:T(128)S(6)} %copy.7), kind=kOutput, calls=%fused_computation.31 | convolution fusion | flops 620977728 | bytes 3671816 | tf_op jit(solution)/shard_map/dot_general | solution.py:58
  158.4 3.5 %fusion.71 = f32[448,768]{1,0:T(8,128)} fusion(bf16[896,768]{1,0:T(8,128)(2,1)} %collective-permute-done.3, f32[448,896]{1,0:T(8,128)S(1)} %get-tuple-element.10, f32[]{:T(128)S(6)} %copy.7), kind=kOutput, calls=%fused_computation.106 | convolution fusion | flops 618168320 | bytes 4358148 | tf_op jit(solution)/shard_map/dot_general | solution.py:101
  161.9 0.0 collective-permute-done.9
  162.0 4.6 %fusion.38 = f32[448,768]{1,0:T(8,128)} fusion(bf16[896,768]{1,0:T(8,128)(2,1)} %collective-permute-done.9, bf16[448,768]{1,0:T(8,128)(2,1)S(1)} %get-tuple-element.21, f32[]{:T(128)S(6)} %copy.8, f32[]{:T(128)S(6)} %copy.7), kind=kOutput, calls=%fused_computation.74 | convolution fusion | flops 1235935232 | bytes 3440648 | tf_op jit(solution)/shard_map/dot_general | solution.py:103
  166.6 0.0 collective-permute-done.5
  166.6 3.9 %fusion.19 = (f32[448]{0:T(512)S(1)}, f32[448,896]{1,0:T(8,128)}) fusion(f32[]{:T(128)S(6)} %copy.8, bf16[448,768]{1,0:T(8,128)(2,1)S(1)} %get-tuple-element.22, bf16[896,768]{1,0:T(8,128)(2,1)} %collective-permute-done.5, f32[]{:T(128)S(6)} %copy.7), kind=kOutput, calls=%fused_computation.32 | convolution fusion | flops 620977728 | bytes 3671816 | tf_op jit(solution)/shard_map/dot_general | solution.py:58
  170.5 0.0 collective-permute-done.10
  170.5 4.7 %fusion.39 = f32[448,768]{1,0:T(8,128)} fusion(bf16[896,768]{1,0:T(8,128)(2,1)} %collective-permute-done.10, bf16[448,768]{1,0:T(8,128)(2,1)S(1)} %get-tuple-element.21, f32[]{:T(128)S(6)} %copy.8, f32[]{:T(128)S(6)} %copy.7), kind=kOutput, calls=%fused_computation.75 | convolution fusion | flops 1235935232 | bytes 3440648 | tf_op jit(solution)/shard_map/dot_general | solution.py:103
  175.2 5.1 %convolution_add_fusion.1 = f32[448,768]{1,0:T(8,128)} fusion(f32[448,768]{1,0:T(8,128)} %fusion.36, bf16[896,768]{1,0:T(8,128)(2,1)} %fusion.25, bf16[448,768]{1,0:T(8,128)(2,1)S(1)} %get-tuple-element.21, f32[]{:T(128)S(6)} %copy.8, f32[]{:T(128)S(6)} %copy.7, s32[448]{0:T(512)S(1)} %iota_add_fusion), kind=kOutput, calls=%fused_computation.53 | convolution fusion | flops 1237884928 | bytes 4818696 | tf_op jit(solution)/shard_map/dot_general | solution.py:103
  180.4 26.2 %collective-permute-done.7 = bf16[896,768]{1,0:T(8,128)(2,1)} collective-permute-done((bf16[896,768]{1,0:T(8,128)(2,1)}, bf16[896,768]{1,0:T(8,128)(2,1)}, u32[]{:S(2)}, u32[]{:S(2)}) %collective-permute-start.7) | collective-permute-done | bytes 1376288 | tf_op jit(solution)/shard_map/ppermute | solution.py:94
  206.6 6.3 %fusion.30 = (f32[448]{0:T(512)S(1)}, f32[448,768]{1,0:T(8,128)}) fusion(bf16[448,768]{1,0:T(8,128)(2,1)S(1)} %copy-done, f32[448]{0:T(512)S(1)} %add_rsqrt_fusion, f32[448,768]{1,0:T(8,128)} %fusion.39, f32[448,768]{1,0:T(8,128)} %fusion.38, f32[448,768]{1,0:T(8,128)} %fusion.37, f32[448,768]{1,0:T(8,128)} %convolution_add_fusion.1, ...), kind=kOutput, calls=%fused_computation.66 | convolution fusion | flops 1238687232 | bytes 9637384 | tf_op jit(solution)/shard_map/dot_general | solution.py:103
  212.9 0.0 copy-start.3
  212.9 2.8 %fusion.32 = f32[448,768]{1,0:T(8,128)} fusion(f32[448,768]{1,0:T(8,128)} %get-tuple-element.20, bf16[448,768]{1,0:T(8,128)(2,1)S(1)} %copy-done, f32[448]{0:T(512)S(1)} %get-tuple-element.19, f32[448]{0:T(512)S(1)} %add_rsqrt_fusion), kind=kLoop, calls=%fused_computation.68 | loop fusion | flops 1720320 | bytes 3444224 | tf_op jit(solution)/shard_map/mul | solution.py:20
  215.7 0.0 copy-done.3
  215.7 0.0 copy-start.4
  215.7 2.5 %fusion.72 = f32[448,768]{1,0:T(8,128)S(1)} fusion(bf16[896,768]{1,0:T(8,128)(2,1)} %collective-permute-done.4, f32[448,896]{1,0:T(8,128)S(1)} %copy-done.3, f32[]{:T(128)S(6)} %copy.7), kind=kOutput, calls=%fused_computation.107 | convolution fusion | flops 618168320 | bytes 4358148 | tf_op jit(solution)/shard_map/dot_general | solution.py:101
  218.2 0.0 copy-done.4
  218.2 0.0 copy-start.5
  218.3 0.0 copy-start.6
  218.3 2.5 %fusion.73 = f32[448,768]{1,0:T(8,128)S(1)} fusion(bf16[896,768]{1,0:T(8,128)(2,1)} %collective-permute-done.5, f32[448,896]{1,0:T(8,128)S(1)} %copy-done.4, f32[]{:T(128)S(6)} %copy.7), kind=kOutput, calls=%fused_computation.108 | convolution fusion | flops 618168320 | bytes 4358148 | tf_op jit(solution)/shard_map/dot_general | solution.py:101
  220.8 0.0 copy-done.5
  220.8 0.0 copy-done.6
  220.8 2.8 %convolution_add_fusion.3 = f32[448,768]{1,0:T(8,128)S(1)} fusion(f32[448,768]{1,0:T(8,128)S(1)} %copy-done.5, bf16[896,768]{1,0:T(8,128)(2,1)} %fusion.24, f32[448,896]{1,0:T(8,128)S(1)} %copy-done.6, f32[]{:T(128)S(6)} %copy.7, s32[448]{0:T(512)S(1)} %iota_add_fusion), kind=kOutput, calls=%fused_computation.55 | convolution fusion | flops 620118016 | bytes 5736196 | tf_op jit(solution)/shard_map/dot_general | solution.py:101
  223.7 0.0 copy-start.2
  223.7 0.0 collective-permute-done.2
  223.7 3.1 %fusion.16 = (f32[448]{0:T(512)S(1)}, f32[448,896]{1,0:T(8,128)S(1)}) fusion(f32[]{:T(128)S(6)} %copy.8, bf16[448,768]{1,0:T(8,128)(2,1)S(1)} %get-tuple-element.22, bf16[896,768]{1,0:T(8,128)(2,1)} %collective-permute-done.2, f32[]{:T(128)S(6)} %copy.7), kind=kOutput, calls=%fused_computation.29 | convolution fusion | flops 620977728 | bytes 3671816 | tf_op jit(solution)/shard_map/dot_general | solution.py:58
  226.8 0.0 copy-done.2
  226.8 2.7 %fusion.26 = (f32[448]{0:T(512)S(1)}, f32[448,768]{1,0:T(8,128)S(1)}) fusion(bf16[448,768]{1,0:T(8,128)(2,1)S(1)} %copy-done.1, f32[448]{0:T(512)S(1)} %add_rsqrt_fusion.1, f32[448,768]{1,0:T(8,128)S(1)} %fusion.73, f32[448,768]{1,0:T(8,128)S(1)} %fusion.72, f32[448,768]{1,0:T(8,128)S(1)} %copy-done.2, f32[448,768]{1,0:T(8,128)S(1)} %convolution_add_fusion.3, ...), kind=kOutput, calls=%fused_computation.62 | convolution fusion | flops 620920384 | bytes 10554884 | tf_op jit(solution)/shard_map/dot_general | solution.py:101
  229.5 1.4 fusion.28
  230.9 0.6 add_multiply_fusion.5
  (3 shorter events, 0.0 us)
Async XLA Ops:
  0.6 2.8 %copy-start = (bf16[448,768]{1,0:T(8,128)(2,1)S(1)}, bf16[448,768]{1,0:T(8,128)(2,1)}, u32[]{:S(2)}) copy-start(bf16[448,768]{1,0:T(8,128)(2,1)} %param.5) | copy-start | bytes 2064388
  0.6 2.8 %copy-start.1 = (bf16[448,768]{1,0:T(8,128)(2,1)S(1)}, bf16[448,768]{1,0:T(8,128)(2,1)}, u32[]{:S(2)}) copy-start(bf16[448,768]{1,0:T(8,128)(2,1)} %param.4) | copy-start | bytes 2064388
  4.9 31.4 %collective-permute-start = (bf16[896,768]{1,0:T(8,128)(2,1)}, bf16[896,768]{1,0:T(8,128)(2,1)}, u32[]{:S(2)}, u32[]{:S(2)}) collective-permute-start(bf16[896,768]{1,0:T(8,128)(2,1)} %pad_maximum_fusion.1), channel_id=1, source_target_pairs={{0,1},{1,0},{2,3},{3,2},{4,5},{5,4},{6,7},{7,6},{8,9},{9,8},{10,11... | collective-permute-start | bytes 4128776 | tf_op jit(solution)/shard_map/ppermute | solution.py:87
  39.3 46.1 %collective-permute-start.6 = (bf16[896,768]{1,0:T(8,128)(2,1)}, bf16[896,768]{1,0:T(8,128)(2,1)}, u32[]{:S(2)}, u32[]{:S(2)}) collective-permute-start(bf16[896,768]{1,0:T(8,128)(2,1)} %fusion.25), channel_id=1, source_target_pairs={{0,255},{1,254},{2,0},{3,1},{4,3},{5,2},{6,4},{7,5},{8,7},{9,6},{1... | collective-permute-start | bytes 4128776 | tf_op jit(solution)/shard_map/ppermute | solution.py:94
  42.5 73.1 %collective-permute-start.1 = (bf16[896,768]{1,0:T(8,128)(2,1)}, bf16[896,768]{1,0:T(8,128)(2,1)}, u32[]{:S(2)}, u32[]{:S(2)}) collective-permute-start(bf16[896,768]{1,0:T(8,128)(2,1)} %fusion.24), channel_id=1, source_target_pairs={{0,2},{1,3},{2,5},{3,4},{4,6},{5,7},{6,9},{7,8},{8,10},{9,11},{10,... | collective-permute-start | bytes 4128776 | tf_op jit(solution)/shard_map/ppermute | solution.py:93
  45.2 75.7 %collective-permute-start.8 = (bf16[896,768]{1,0:T(8,128)(2,1)}, bf16[896,768]{1,0:T(8,128)(2,1)}, u32[]{:S(2)}, u32[]{:S(2)}) collective-permute-start(bf16[896,768]{1,0:T(8,128)(2,1)} %fusion.25), channel_id=1, source_target_pairs={{0,250},{1,251},{2,253},{3,252},{4,254},{5,255},{6,1},{7,0},{8,2},... | collective-permute-start | bytes 4128776 | tf_op jit(solution)/shard_map/ppermute | solution.py:94
  47.2 114.7 %collective-permute-start.9 = (bf16[896,768]{1,0:T(8,128)(2,1)}, bf16[896,768]{1,0:T(8,128)(2,1)}, u32[]{:S(2)}, u32[]{:S(2)}) collective-permute-start(bf16[896,768]{1,0:T(8,128)(2,1)} %fusion.25), channel_id=1, source_target_pairs={{0,248},{1,249},{2,250},{3,251},{4,252},{5,253},{6,254},{7,255},{8... | collective-permute-start | bytes 4128776 | tf_op jit(solution)/shard_map/ppermute | solution.py:94
  47.6 123.0 %collective-permute-start.10 = (bf16[896,768]{1,0:T(8,128)(2,1)}, bf16[896,768]{1,0:T(8,128)(2,1)}, u32[]{:S(2)}, u32[]{:S(2)}) collective-permute-start(bf16[896,768]{1,0:T(8,128)(2,1)} %fusion.25), channel_id=1, source_target_pairs={{0,247},{1,246},{2,248},{3,249},{4,251},{5,250},{6,252},{7,253},{8... | collective-permute-start | bytes 4128776 | tf_op jit(solution)/shard_map/ppermute | solution.py:94
  85.4 44.1 %collective-permute-start.3 = (bf16[896,768]{1,0:T(8,128)(2,1)}, bf16[896,768]{1,0:T(8,128)(2,1)}, u32[]{:S(2)}, u32[]{:S(2)}) collective-permute-start(bf16[896,768]{1,0:T(8,128)(2,1)} %fusion.24), channel_id=1, source_target_pairs={{0,7},{1,6},{2,8},{3,9},{4,11},{5,10},{6,12},{7,13},{8,15},{9,14},... | collective-permute-start | bytes 4128776 | tf_op jit(solution)/shard_map/ppermute | solution.py:93
  115.7 20.2 %collective-permute-start.4 = (bf16[896,768]{1,0:T(8,128)(2,1)}, bf16[896,768]{1,0:T(8,128)(2,1)}, u32[]{:S(2)}, u32[]{:S(2)}) collective-permute-start(bf16[896,768]{1,0:T(8,128)(2,1)} %fusion.24), channel_id=1, source_target_pairs={{0,8},{1,9},{2,10},{3,11},{4,12},{5,13},{6,14},{7,15},{8,16},{9,17... | collective-permute-start | bytes 4128776 | tf_op jit(solution)/shard_map/ppermute | solution.py:93
  120.9 85.7 %collective-permute-start.7 = (bf16[896,768]{1,0:T(8,128)(2,1)}, bf16[896,768]{1,0:T(8,128)(2,1)}, u32[]{:S(2)}, u32[]{:S(2)}) collective-permute-start(bf16[896,768]{1,0:T(8,128)(2,1)} %fusion.25), channel_id=1, source_target_pairs={{0,253},{1,252},{2,255},{3,254},{4,1},{5,0},{6,3},{7,2},{8,5},{9,4... | collective-permute-start | bytes 4128776 | tf_op jit(solution)/shard_map/ppermute | solution.py:94
  129.5 37.1 %collective-permute-start.5 = (bf16[896,768]{1,0:T(8,128)(2,1)}, bf16[896,768]{1,0:T(8,128)(2,1)}, u32[]{:S(2)}, u32[]{:S(2)}) collective-permute-start(bf16[896,768]{1,0:T(8,128)(2,1)} %fusion.24), channel_id=1, source_target_pairs={{0,10},{1,11},{2,13},{3,12},{4,14},{5,15},{6,17},{7,16},{8,18},{9,... | collective-permute-start | bytes 4128776 | tf_op jit(solution)/shard_map/ppermute | solution.py:93
  135.9 87.8 %collective-permute-start.2 = (bf16[896,768]{1,0:T(8,128)(2,1)}, bf16[896,768]{1,0:T(8,128)(2,1)}, u32[]{:S(2)}, u32[]{:S(2)}) collective-permute-start(bf16[896,768]{1,0:T(8,128)(2,1)} %fusion.24), channel_id=1, source_target_pairs={{0,5},{1,4},{2,7},{3,6},{4,9},{5,8},{6,11},{7,10},{8,13},{9,12},{1... | collective-permute-start | bytes 4128776 | tf_op jit(solution)/shard_map/ppermute | solution.py:93
  212.9 2.8 %copy-start.3 = (f32[448,896]{1,0:T(8,128)S(1)}, f32[448,896]{1,0:T(8,128)}, u32[]{:S(2)}) copy-start(f32[448,896]{1,0:T(8,128)} %get-tuple-element.8) | copy-start | bytes 4816900
  215.7 2.5 %copy-start.4 = (f32[448,896]{1,0:T(8,128)S(1)}, f32[448,896]{1,0:T(8,128)}, u32[]{:S(2)}) copy-start(f32[448,896]{1,0:T(8,128)} %get-tuple-element.6) | copy-start | bytes 4816900
  218.2 2.6 %copy-start.5 = (f32[448,768]{1,0:T(8,128)S(1)}, f32[448,768]{1,0:T(8,128)}, u32[]{:S(2)}) copy-start(f32[448,768]{1,0:T(8,128)} %fusion.70) | copy-start | bytes 4128772
  218.3 2.6 %copy-start.6 = (f32[448,896]{1,0:T(8,128)S(1)}, f32[448,896]{1,0:T(8,128)}, u32[]{:S(2)}) copy-start(f32[448,896]{1,0:T(8,128)} %get-tuple-element.14) | copy-start | bytes 4816900
  223.7 3.1 %copy-start.2 = (f32[448,768]{1,0:T(8,128)S(1)}, f32[448,768]{1,0:T(8,128)}, u32[]{:S(2)}) copy-start(f32[448,768]{1,0:T(8,128)} %fusion.71) | copy-start | bytes 4128772
